TPU v7x, 32 devices: a whole 2x2x4 slice. The times are simulated.
32 devices in a mesh: groups: 2 (over y), leaf: 4 (over z), state: 2 (over x), sub: 2 (over core).
Axes of the slice: x: 2, y: 2, z: 4, core: 2. Of those that a mesh axis runs over, the one named last changes fastest.
Arguments:
- sphere_coef: bfloat16 [12, 25, 2, 2, 4, 2048], P(None, None, None, None, None, ('groups', 'leaf', 'state', 'sub')), parts along dimension 5, may hold values from -6 to 6
- live_blocks: int32 [32], P(('groups', 'leaf', 'state', 'sub')), parts along dimension 0, may hold values from 1 to 4, as said below
- cluster: int32 [2048], P(('groups', 'leaf', 'state', 'sub')), parts along dimension 0, may hold values from 0 to 15
- leaf_parent: int32 [512], P(('groups', 'leaf', 'state', 'sub')), parts along dimension 0, may hold values from 0 to 1
- leaf_octant: int32 [512], P(('groups', 'leaf', 'state', 'sub')), parts along dimension 0, may hold values from 0 to 7
- box_octant: int32 [64], P(('groups', 'leaf', 'state', 'sub')), parts along dimension 0, may hold values from 0 to 7
- rotation: float32 [8, 2, 12, 25, 25], replicated, may hold values from -0.875 to 0.875
- axial_one: float32 [2, 25, 2, 12, 2, 12], replicated, may hold values from -0.3125 to 0.3125
- axial_two: float32 [2, 25, 2, 12, 2, 12], replicated, may hold values from -0.3125 to 0.3125
- owner_rotation: float32 [8, 2, 12, 25, 25], P(('groups', 'leaf')), parts along dimension 0, may hold values from -0.875 to 0.875
- owner_axial: float32 [8, 2, 25, 2, 128, 2, 12], P(('groups', 'leaf'), None, None, None, ('state', 'sub')), parts along dimension 0, may hold values from -0.875 to 0.875
- owner_angle: float32 [8], P('groups'), parts along dimension 0, may hold values from -3.140625 to 3.140625
- turn_table: bfloat16 [8, 128, 25, 256], P(('groups', 'leaf'), ('state', 'sub')), parts along dimension 0, may hold values from -0.625 to 0.625
- angular_table: bfloat16 [256, 128, 32], P('leaf', ('state', 'sub')), may hold values from -0.375 to 0.375
Outputs:
- far_field: float32 [32, 4, 2, 2, 2048], P(('groups', 'leaf', 'state', 'sub')), parts along dimension 0
There are 2 independent parts, one for each index of `groups`. A program takes and returns all parts, laid end to end along the dimension named above; an argument that names none is the same for every part. Nothing has to cross between parts.
Inputs may be any that keep to these rules, and one draw needn't show every extreme that they name: `live_blocks`: live blocks of 16 sphere slots on each device; some device has all 4 live in every draw.
All inputs are finite; a program needn't handle non-finite values.
Results may differ from a plain program's by a relative error of at most 0.018.
Values may be sent and summed in bfloat16 or wider, within the bound.
No kernel may reach another device: no remote copies, remote signals or barrier semaphores. Data moves between devices by JAX's collectives and lax.ppermute only.
A program may use at most 64 MiB of HBM per device.

v0:
```python
import math
import jax
import jax.numpy as jnp
from jax import lax
from jax.sharding import PartitionSpec as P

STATES = 4
SBLK = 4
PHI = 2048


def complex_join(first, second, half):
    real = first[..., :half] - second[..., half:]
    imag = first[..., half:] + second[..., :half]
    return jnp.concatenate([real, imag], axis=-1)


def turn_select(vectors, rotation, octants, backward):
    degrees, orders, width = vectors.shape
    if backward:
        mats = jnp.transpose(rotation, (1, 2, 0, 4, 3))
        sign = -1.0
    else:
        mats = jnp.transpose(rotation, (1, 2, 0, 3, 4))
        sign = 1.0
    mats = mats.reshape(2, degrees, 8 * orders, orders)
    first = jnp.einsum("lQp,lpC->lQC", mats[0], vectors, precision=lax.Precision.HIGHEST)
    second = sign * jnp.einsum("lQp,lpC->lQC", mats[1], vectors, precision=lax.Precision.HIGHEST)
    joined = complex_join(first, second, width // 2).reshape(degrees, 8, orders, width)
    count = octants.shape[0]
    chosen = (octants[None, :] == jnp.arange(8, dtype=jnp.int32)[:, None]).astype(jnp.float32)
    column_mask = jnp.tile(chosen, (1, width // count))
    return jnp.sum(joined * column_mask[None, :, None, :], axis=1)


def axial_apply(vectors, axial):
    degrees, orders, width = vectors.shape
    rest = width // 4
    moved = vectors.reshape(degrees, orders, 2, 2, rest)
    moved = jnp.transpose(moved, (1, 3, 0, 2, 4)).reshape(orders, 2 * degrees, 2 * rest)
    mats = axial.reshape(2, orders, 2 * degrees, 2 * degrees)
    first = jnp.einsum("qab,qbC->qaC", mats[0], moved, precision=lax.Precision.HIGHEST)
    second = jnp.einsum("qab,qbC->qaC", mats[1], moved, precision=lax.Precision.HIGHEST)
    joined = complex_join(first, second, rest).reshape(orders, 2, degrees, 2, rest)
    return jnp.transpose(joined, (2, 0, 3, 1, 4)).reshape(degrees, orders, width)


def move_expansion(vectors, octants, rotation, axial):
    turned = turn_select(vectors, rotation, octants, False)
    return turn_select(axial_apply(turned, axial), rotation, octants, True)


def local_boxes(
    sphere_block,
    live_count,
    cluster,
    leaf_parent,
    leaf_octant,
    box_octant,
    rotation,
    axial_one,
    axial_two,
):
    degrees, orders = (sphere_block.shape[0], sphere_block.shape[1])
    channel = sphere_block.shape[2] * sphere_block.shape[3] * sphere_block.shape[4]
    slots = sphere_block.shape[-1]
    per_block = slots // SBLK
    alive = jnp.arange(slots, dtype=jnp.int32) // per_block < live_count
    leaf_total = leaf_parent.shape[0]
    member = (
        (cluster[:, None] == jnp.arange(leaf_total, dtype=jnp.int32)[None, :]) & alive[:, None]
    ).astype(jnp.bfloat16)
    ident = jnp.eye(channel, dtype=jnp.bfloat16)
    spread = (ident[:, None, :, None] * member[None, :, None, :]).reshape(
        channel * slots, channel * leaf_total
    )
    leaves = jnp.dot(
        sphere_block.reshape(degrees * orders, channel * slots),
        spread,
        preferred_element_type=jnp.float32,
    ).reshape(degrees, orders, channel * leaf_total)
    moved = move_expansion(leaves, leaf_octant, rotation, axial_one)
    box_total = box_octant.shape[0]
    parents = (leaf_parent[:, None] == jnp.arange(box_total, dtype=jnp.int32)[None, :]).astype(
        jnp.float32
    )
    wide_ident = jnp.eye(channel, dtype=jnp.float32)
    wide_parents = (wide_ident[:, None, :, None] * parents[None, :, None, :]).reshape(
        channel * leaf_total, channel * box_total
    )
    boxes = jnp.einsum("lpC,CD->lpD", moved, wide_parents, precision=lax.Precision.HIGHEST)
    outer = move_expansion(boxes, box_octant, rotation, axial_two)
    return outer.reshape(degrees, orders, channel, box_total).sum(-1)


def owner_frame(owner_sum, owner_turn, owner_shift):
    degrees, orders, width = owner_sum.shape
    states = width // 4
    first = jnp.einsum("lqp,lpC->lqC", owner_turn[0], owner_sum, precision=lax.Precision.HIGHEST)
    second = jnp.einsum("lqp,lpC->lqC", owner_turn[1], owner_sum, precision=lax.Precision.HIGHEST)
    turned = complex_join(first, second, width // 2)
    moved = turned.reshape(degrees, orders, 2, 2, states)
    moved = jnp.transpose(moved, (1, 3, 0, 2, 4)).reshape(orders, 2 * degrees, 2 * states)
    root_degrees = owner_shift.shape[3]
    mats = owner_shift.reshape(2, orders, 2 * root_degrees, 2 * degrees)
    first = jnp.einsum("qab,qbC->qaC", mats[0], moved, precision=lax.Precision.HIGHEST)
    second = jnp.einsum("qab,qbC->qaC", mats[1], moved, precision=lax.Precision.HIGHEST)
    joined = complex_join(first, second, states).reshape(orders, 2, root_degrees, 2, states)
    framed = jnp.transpose(joined, (2, 1, 3, 4, 0)).reshape(root_degrees, 4 * states, orders)
    return framed.astype(jnp.bfloat16)


def rotate_back(framed, functions, azimuth, half_orders):
    root_degrees, width = (framed.shape[0], framed.shape[1])
    states = width // 4
    orders_here = functions.shape[2]
    values = jnp.einsum("nCm,nmj->nCj", framed, functions, preferred_element_type=jnp.float32)
    values = values.reshape(root_degrees, 2, 2, states, orders_here)
    order_values = (jnp.arange(orders_here, dtype=jnp.int32) - half_orders).astype(jnp.float32)
    cosine = jnp.cos(order_values * azimuth)
    sine = jnp.sin(order_values * azimuth)
    real_part = cosine * values[:, :, 0] + sine * values[:, :, 1]
    imag_part = cosine * values[:, :, 1] - sine * values[:, :, 0]
    joined = jnp.stack([real_part, imag_part], axis=2)
    return jnp.transpose(joined, (4, 1, 2, 3, 0)).reshape(orders_here, 4 * states * root_degrees)


def legendre_field(root_coef, table):
    orders_here, root_degrees = (table.shape[0], table.shape[1])
    lat_total = table.shape[2] // 2
    rows = root_coef.shape[1] // root_degrees
    states = rows // 4
    half = rows // 2
    blocks = jnp.einsum(
        "jrn,jnK->jrK",
        root_coef.reshape(orders_here, rows, root_degrees),
        table,
        preferred_element_type=jnp.float32,
    )
    theta_part = blocks[:, :half, :lat_total] + blocks[:, half:, lat_total:]
    cross = blocks[:, :half, lat_total:] + blocks[:, half:, :lat_total]
    phi_part = jnp.concatenate([-cross[:, states:], cross[:, :states]], axis=1)
    return jnp.concatenate([theta_part, phi_part], axis=1)


def phase_table(orders, longitudes):
    order_ids = jnp.arange(orders, dtype=jnp.int32) - orders // 2
    column = jnp.arange(2 * longitudes, dtype=jnp.int32)
    along = column % longitudes
    quarter = (column // longitudes).astype(jnp.float32)
    remainder = jnp.mod(order_ids[:, None] * along[None, :], longitudes)
    phase = remainder.astype(jnp.float32) * (2.0 * math.pi / longitudes) - quarter[None, :] * (
        0.5 * math.pi
    )
    return jnp.cos(phase).astype(jnp.bfloat16)


def synthesize(spectrum, longitudes, states):
    orders = spectrum.shape[1]
    table = phase_table(orders, longitudes)
    product = jnp.dot(spectrum, table, preferred_element_type=jnp.float32)
    product = product.reshape(2, 2, states, -1, 2 * longitudes)
    real_part = product[:, 0, :, :, :longitudes] - product[:, 1, :, :, longitudes:]
    imag_part = product[:, 0, :, :, longitudes:] + product[:, 1, :, :, :longitudes]
    joined = jnp.stack([real_part, imag_part], axis=3)
    return jnp.transpose(joined, (2, 1, 0, 3, 4)) * (1.0 / math.sqrt(orders))


def on_device(
    sphere_coef,
    live_blocks,
    cluster,
    leaf_parent,
    leaf_octant,
    box_octant,
    rotation,
    axial_one,
    axial_two,
    owner_rotation,
    owner_axial,
    owner_angle,
    turn_table,
    angular_table,
):
    partial_owner = local_boxes(
        sphere_coef,
        live_blocks[0],
        cluster,
        leaf_parent,
        leaf_octant,
        box_octant,
        rotation,
        axial_one,
        axial_two,
    )
    owner_sum = lax.psum(partial_owner, ("state", "sub"))
    framed = owner_frame(owner_sum, owner_rotation[0], owner_axial[0])
    leaf_size = lax.axis_size("leaf")
    orders = turn_table.shape[3]
    half_orders = orders // 2
    own_orders = orders // leaf_size
    own_azimuth = owner_angle[lax.axis_index("leaf")]
    piece = turn_table[0]
    root = lax.psum_scatter(
        rotate_back(framed, piece, own_azimuth, half_orders),
        "leaf",
        scatter_dimension=0,
        tiled=True,
    )
    root_coef = root.astype(jnp.bfloat16)
    field = legendre_field(root_coef, angular_table)
    channel = field.shape[1]
    group_size = lax.axis_size("state") * lax.axis_size("sub")
    lat_rows = field.shape[2] // (leaf_size * group_size)
    shaped = field.reshape(own_orders, channel, leaf_size, group_size, lat_rows)
    shaped = jnp.transpose(shaped, (3, 2, 1, 4, 0)).reshape(
        group_size, leaf_size, channel * lat_rows * own_orders
    )
    summed = lax.psum_scatter(
        shaped.astype(jnp.bfloat16), ("state", "sub"), scatter_dimension=0, tiled=True
    )
    moved = lax.all_to_all(summed, "leaf", split_axis=1, concat_axis=2, tiled=True)
    spectrum = moved.reshape(leaf_size, channel, lat_rows, own_orders)
    spectrum = jnp.transpose(spectrum, (1, 2, 0, 3)).reshape(channel * lat_rows, orders)
    return synthesize(spectrum, PHI, STATES)


def solution(mesh):
    return jax.shard_map(
        on_device,
        mesh=mesh,
        in_specs=(
            P(None, None, None, None, None, ("groups", "leaf", "state", "sub")),
            P(("groups", "leaf", "state", "sub")),
            P(("groups", "leaf", "state", "sub")),
            P(("groups", "leaf", "state", "sub")),
            P(("groups", "leaf", "state", "sub")),
            P(("groups", "leaf", "state", "sub")),
            P(),
            P(),
            P(),
            P(("groups", "leaf"), None, None, None, None),
            P(("groups", "leaf"), None, None, None, ("state", "sub"), None, None),
            P("groups"),
            P(("groups", "leaf"), ("state", "sub"), None, None),
            P("leaf", ("state", "sub"), None),
        ),
        out_specs=P(("groups", "leaf", "state", "sub"), None, None, None, None),
        check_vma=False,
    )
```

profile of v0, /device:TPU:0, one launch (start us, length us, event | category | flops | bytes accessed | tf_op | source)
XLA Modules:
  0.0 170.0 jit_solution(8647744957523525391)
XLA Ops:
  6.5 0.6 fusion.33
  7.1 4.5 %fusion.46 = (f32[1,12,8,25,25]{4,0,3,1,2:T(1,128)S(1)}, f32[1,12,8,25,25]{4,0,3,1,2:T(1,128)S(1)}) fusion(f32[2,12,8,25,25]{4,0,3,1,2:T(2,128)} %bitcast.182), kind=kLoop, calls=%fused_computation.129 | loop fusion | bytes 960000 | tf_op jit(solution)/shard_map/slice | solution.py:27
  11.7 2.4 %copy.163 = f32[1,12,8,25,25]{3,2,4,1,0:T(8,128)} copy(f32[1,12,8,25,25]{4,0,3,1,2:T(1,128)S(1)} %get-tuple-element.12) | data formatting | bytes 480000 | tf_op jit(solution)/shard_map/slice | solution.py:28
  14.1 2.4 %squeeze.61 = f32[12,200,25]{1,2,0:T(8,128)} reshape(f32[1,12,8,25,25]{3,2,4,1,0:T(8,128)} %copy.163) | data formatting | bytes 480000 | tf_op jit(solution)/shard_map/squeeze | solution.py:28
  17.4 0.7 mul.178
  18.1 2.6 %reshape.344 = bf16[300,1024]{1,0:T(8,128)(2,1)S(1)} reshape(bf16[12,25,2,2,4,64]{5,4,3,2,1,0:T(4,128)(2,1)} %param.14) | data formatting | bytes 1228800 | tf_op jit(solution)/shard_map/reshape | solution.py:78
  21.2 1.1 copy.162
  22.7 3.3 %convolution_bitcast_fusion.2 = f32[12,200,256]{2,1,0:T(8,128)S(1)} fusion(f32[12,25,256]{2,1,0:T(8,128)S(1)} %reshape.345, f32[12,200,25]{1,2,0:T(8,128)} %squeeze.61), kind=kOutput, calls=%fused_computation.26 | convolution fusion | flops 184320000 | bytes 3004800 | tf_op jit(solution)/shard_map/lQp,lpC->lQC/dot_general | solution.py:28
  26.0 2.2 %convolution_bitcast_fusion.3 = f32[12,200,256]{2,1,0:T(8,128)S(1)} fusion(f32[12,25,256]{2,1,0:T(8,128)S(1)} %reshape.345, f32[12,200,25]{1,2,0:T(8,128)S(1)} %squeeze.60), kind=kOutput, calls=%fused_computation.27 | convolution fusion | flops 184320000 | bytes 3004800 | tf_op jit(solution)/shard_map/lQp,lpC->lQC/dot_general | solution.py:27
  28.4 1.6 pad_maximum_fusion
  30.1 2.5 %reshape.346 = f32[12,8,25,256]{3,2,1,0:T(8,128)S(1)} reshape(f32[12,200,256]{2,1,0:T(8,128)} %pad_maximum_fusion) | data formatting | bytes 4915200 | tf_op jit(solution)/shard_map/reshape | solution.py:29
  32.5 0.7 fusion.37
  33.2 0.6 tile.8
  33.8 1.5 tile.9
  35.4 1.9 %multiply_reduce_fusion.1 = f32[12,25,256]{2,1,0:T(8,128)} fusion(f32[12,8,25,256]{3,2,1,0:T(8,128)S(1)} %reshape.346, f32[8,256]{1,0:T(8,128)} %tile.9), kind=kLoop, calls=%fused_computation.13 | loop fusion | flops 1152000 | bytes 2772992 | tf_op jit(solution)/shard_map/reduce_sum | solution.py:33
  37.2 1.4 reshape.347
  39.4 0.7 copy.206
  40.4 1.1 copy.205
  41.8 0.6 convolution_bitcast_fusion.8
  42.5 0.6 convolution_bitcast_fusion.9
  43.5 1.2 reshape.349
  44.7 2.2 %copy.169 = f32[12,25,2,2,64]{4,3,2,1,0:T(2,128)} copy(f32[12,25,2,2,64]{4,2,0,3,1:T(2,128)} %bitcast.184) | data formatting | bytes 614400 | tf_op jit(solution)/shard_map/transpose | solution.py:45
  46.9 1.5 reshape.350
  48.4 2.9 %fusion.45 = (f32[1,12,8,25,25]{3,0,4,1,2:T(1,128)S(1)}, f32[1,12,8,25,25]{3,0,4,1,2:T(1,128)}) fusion(f32[2,12,8,25,25]{3,0,4,1,2:T(2,128)S(1)} %bitcast.183), kind=kLoop, calls=%fused_computation.128 | loop fusion | bytes 960000 | tf_op jit(solution)/shard_map/slice | solution.py:27
  51.5 1.1 squeeze.64
  53.1 3.3 %convolution_bitcast_fusion.1 = f32[12,200,256]{2,1,0:T(8,128)S(1)} fusion(f32[12,25,256]{2,1,0:T(8,128)S(1)} %reshape.350, f32[12,200,25]{1,2,0:T(8,128)} %squeeze.64), kind=kOutput, calls=%fused_computation.25 | convolution fusion | flops 184320000 | bytes 3004800 | tf_op jit(solution)/shard_map/lQp,lpC->lQC/dot_general | solution.py:27
  56.5 2.2 %multiply_bitcast_fusion = f32[12,200,256]{2,1,0:T(8,128)S(1)} fusion(f32[12,25,256]{2,1,0:T(8,128)S(1)} %reshape.350, f32[12,200,25]{1,2,0:T(8,128)S(1)} %squeeze.65), kind=kOutput, calls=%fused_computation.16 | convolution fusion | flops 184934400 | bytes 3004800 | tf_op jit(solution)/shard_map/lQp,lpC->lQC/dot_general | solution.py:28
  58.9 1.6 pad_maximum_fusion.1
  60.5 2.6 %reshape.351 = f32[12,8,25,256]{3,2,1,0:T(8,128)S(1)} reshape(f32[12,200,256]{2,1,0:T(8,128)} %pad_maximum_fusion.1) | data formatting | bytes 4915200 | tf_op jit(solution)/shard_map/reshape | solution.py:29
  63.2 1.9 %multiply_reduce_fusion = f32[12,25,256]{2,1,0:T(8,128)} fusion(f32[12,8,25,256]{3,2,1,0:T(8,128)S(1)} %reshape.351, f32[8,256]{1,0:T(8,128)} %tile.9), kind=kLoop, calls=%fused_computation.12 | loop fusion | flops 1152000 | bytes 2772992 | tf_op jit(solution)/shard_map/reduce_sum | solution.py:33
  65.3 2.0 %fusion.51 = f32[12,25,32]{1,2,0:T(8,128)S(1)} fusion(f32[12,25,256]{2,1,0:T(8,128)} %multiply_reduce_fusion, f32[256,32,1]{0,1,2:T(8,128)S(1)} %reshape.365), kind=kOutput, calls=%fused_computation.136 | convolution fusion | flops 29491200 | bytes 378368 | tf_op jit(solution)/shard_map/lpC,CD->lpD/dot_general | solution.py:91
  67.3 1.5 convolution_bitcast_fusion.6
  68.8 1.5 convolution_bitcast_fusion.5
  70.4 0.5 reshape.352
  71.0 0.5 multiply_reduce_fusion.3
  71.8 0.7 copy.208
  72.8 0.7 copy.207
  73.8 0.6 convolution_bitcast_fusion.10
  74.4 0.6 convolution_bitcast_fusion.11
  75.3 0.5 convolution_bitcast_fusion.4
  75.8 0.5 fusion.15
  76.4 0.5 reshape.357
  76.9 0.5 multiply_reduce_fusion.2
  77.7 13.9 %psum.7 = f32[12,25,16]{1,2,0:T(8,128)S(1)} all-reduce(f32[12,25,16]{1,2,0:T(8,128)S(1)} %reduce_sum.49), channel_id=1, replica_groups=mesh['groups'=2,'leaf'=4,'state'=2,'sub'=2] {'state','sub'}, use_global_device_ids=true, to_apply=%region_5.6 | all-reduce | flops 4800 | bytes 38400 | tf_op jit(solution)/shard_map/psum | solution.py:196
  91.6 1.4 fusion.50
  93.0 0.4 convolution_bitcast_fusion.14
  93.4 0.4 convolution_bitcast_fusion.15
  95.9 0.4 convolution_bitcast_fusion.13
  97.5 0.6 dynamic_slice.3
  98.0 0.7 fusion.38
  98.9 1.0 copy.210
  99.9 0.8 copy.195
  100.7 0.6 dynamic-slice
  101.3 20.8 %reduce-scatter.4.cloned.1.call-done = f32[64,512]{1,0:T(8,128)} async-done(((f32[256,512]{1,0:T(8,128)}), f32[64,512]{1,0:T(8,128)}) %reduce-scatter.4.cloned.1.call-update) | async-done | bytes 131088
  122.0 1.0 copy.211
  124.5 10.3 %all-reduce = bf16[4,4,1024]{2,1,0:T(4,128)(2,1)S(1)} all-reduce(bf16[4,4,1024]{2,1,0:T(4,128)(2,1)S(1)} %copy.209), channel_id=3, replica_groups=mesh['groups'=2,'leaf'=4,'state'=2,'sub'=2] {'state','sub'}, use_global_device_ids=true, to_apply=%region_7.8.clone | all-reduce | flops 16384 | bytes 65536
  134.7 0.7 constant_dynamic-slice_fusion
  135.4 0.5 broadcast.208
  135.9 0.7 reduce.2
  136.6 0.6 reshape.377
  137.3 3.5 %all-to-all-start = ((bf16[4,2,512]{2,1,0:T(2,128)(2,1)}), bf16[4,2,512]{2,1,0:T(2,128)(2,1)S(1)}, u32[]{:S(2)}, u32[]{:S(2)}) async-start(bf16[4,2,512]{2,1,0:T(2,128)(2,1)} %reshape.377), calls=%async_computation | async-start | bytes 16384 | tf_op jit(solution)/shard_map/all_to_all | solution.py:222
  140.7 5.3 %all-to-all-done = bf16[4,2,512]{2,1,0:T(2,128)(2,1)S(1)} async-done(((bf16[4,2,512]{2,1,0:T(2,128)(2,1)}), bf16[4,2,512]{2,1,0:T(2,128)(2,1)S(1)}, u32[]{:S(2)}, u32[]{:S(2)}) %all-to-all-start) | async-done | bytes 8224 | tf_op jit(solution)/shard_map/all_to_all | solution.py:222
  146.3 15.7 %convolution_bitcast_fusion = f32[2,2,4,1,4096]{4,2,1,0,3:T(4,128)S(1)} fusion(bf16[2,2,4,256]{3,2,1,0:T(4,128)(2,1)S(1)} %dot_general.132, f32[4096]{0:T(1024)S(1)} %fusion.28, s32[4096]{0:T(1024)S(1)} %add_select_fusion.2, s32[256]{0:T(256)S(1)} %iota_add_fusion), kind=kOutput, calls=%fused_computation.5 | convolution fusion | flops 50331648 | bytes 304128 | tf_op jit(solution)/shard_map/dot_general | solution.py:161
  162.1 0.8 copy.202
  (113 shorter events, 10.7 us)
Async XLA Ops:
  6.5 90.2 %copy-start = (bf16[1,32,25,256]{3,1,2,0:T(8,128)(2,1)S(1)}, bf16[1,32,25,256]{3,1,2,0:T(8,128)(2,1)}, u32[]{:S(2)}) copy-start(bf16[1,32,25,256]{3,1,2,0:T(8,128)(2,1)} %param.26) | copy-start | bytes 1228804
  6.5 115.5 %reduce-scatter.4.cloned.1.call-start = ((), (), s32[]{:S(2)}) async-start(), calls=%async_computation.2 | async-start | bytes 655360
  11.7 5.5 %copy-start.12 = (s32[64]{0:T(128)S(1)}, s32[64]{0:T(128)}, u32[]{:S(2)}) copy-start(s32[64]{0:T(128)} %param.16) | copy-start | bytes 772
  22.7 5.5 %copy-start.3 = (f32[12,200,25]{1,2,0:T(8,128)}, f32[12,200,25]{1,2,0:T(8,128)S(1)}, u32[]{:S(2)}) copy-start(f32[12,200,25]{1,2,0:T(8,128)S(1)} %squeeze.60) | copy-start | bytes 720004
  37.2 2.1 %copy-start.8 = (f32[2,25,2,12,2,12]{1,4,5,3,2,0:T(2,128)S(1)}, f32[2,25,2,12,2,12]{1,4,5,3,2,0:T(2,128)}, u32[]{:S(2)}) copy-start(f32[2,25,2,12,2,12]{1,4,5,3,2,0:T(2,128)} %param.21) | copy-start | bytes 345604
  43.3 5.1 %copy-start.1 = (f32[8,2,12,25,25]{4,1,3,2,0:T(2,128)S(1)}, f32[8,2,12,25,25]{4,1,3,2,0:T(2,128)}, u32[]{:S(2)}) copy-start(f32[8,2,12,25,25]{4,1,3,2,0:T(2,128)} %param.20) | copy-start | bytes 1440004
  51.4 1.3 copy-start.2
  53.1 5.5 %copy-start.5 = (f32[12,200,25]{1,2,0:T(8,128)}, f32[12,200,25]{1,2,0:T(8,128)S(1)}, u32[]{:S(2)}) copy-start(f32[12,200,25]{1,2,0:T(8,128)S(1)} %squeeze.65) | copy-start | bytes 720004
  63.2 1.9 %copy-start.13 = (s32[16]{0:T(128)S(1)}, s32[16]{0:T(128)}, u32[]{:S(2)}) copy-start(s32[16]{0:T(128)} %param.17) | copy-start | bytes 196
  63.2 1.9 %copy-start.11 = (f32[16,16]{0,1:T(8,128)S(1)}, f32[16,16]{0,1:T(8,128)}, u32[]{:S(2)}) copy-start(f32[16,16]{0,1:T(8,128)} %fusion.33) | copy-start | bytes 3076
  68.8 2.1 %copy-start.14 = (s32[2]{0:T(128)S(1)}, s32[2]{0:T(128)}, u32[]{:S(2)}) copy-start(s32[2]{0:T(128)} %param.19) | copy-start | bytes 28
  70.4 1.4 copy-start.9
  72.8 2.5 %copy-start.4 = (f32[12,200,25]{1,2,0:T(8,128)S(1)}, f32[12,200,25]{1,2,0:T(8,128)}, u32[]{:S(2)}) copy-start(f32[12,200,25]{1,2,0:T(8,128)} %squeeze.64) | copy-start | bytes 720004
  73.5 2.3 %copy-start.6 = (f32[12,200,25]{1,2,0:T(8,128)S(1)}, f32[12,200,25]{1,2,0:T(8,128)}, u32[]{:S(2)}) copy-start(f32[12,200,25]{1,2,0:T(8,128)} %copy-done.5) | copy-start | bytes 720004
  76.9 17.2 %copy-start.7 = (f32[1,2,25,2,32,2,12]{4,5,6,3,2,1,0:T(2,128)S(1)}, f32[1,2,25,2,32,2,12]{4,5,6,3,2,1,0:T(2,128)}, u32[]{:S(2)}) copy-start(f32[1,2,25,2,32,2,12]{4,5,6,3,2,1,0:T(2,128)} %param.24) | copy-start | bytes 921604
  95.2 2.3 %copy-start.15 = (f32[4]{0:T(128)S(1)}, f32[4]{0:T(128)}, u32[]{:S(2)}) copy-start(f32[4]{0:T(128)} %param.25) | copy-start | bytes 52
  97.1 2.8 %copy-start.10 = (bf16[64,32,32]{0,2,1:T(8,128)(2,1)S(1)}, bf16[64,32,32]{0,2,1:T(8,128)(2,1)}, u32[]{:S(2)}) copy-start(bf16[64,32,32]{0,2,1:T(8,128)(2,1)} %param.27) | copy-start | bytes 393220
  97.4 3.3 %copy-start.16 = (u32[32]{0:T(128)S(1)}, u32[32]{0:T(128)}, u32[]{:S(2)}) copy-start(u32[32]{0:T(128)} %constant.84) | copy-start | bytes 388
  137.3 8.8 %all-to-all-start = ((bf16[4,2,512]{2,1,0:T(2,128)(2,1)}), bf16[4,2,512]{2,1,0:T(2,128)(2,1)S(1)}, u32[]{:S(2)}, u32[]{:S(2)}) async-start(bf16[4,2,512]{2,1,0:T(2,128)(2,1)} %reshape.377), calls=%async_computation | async-start | bytes 16384 | tf_op jit(solution)/shard_map/all_to_all | solution.py:222
Sparse Core Ops, SparseCore 0:
  100.0 22.0 reduce-scatter.3
where the time goes:
time: 173 us; the launch traced here: 170 us
  local copies, waits for them, and re-layouts  50.4 us (29%)
  matrix products  37.5 us (22%)
  waiting for transfers between devices  26.1 us (15%)
  blocking collectives  24.2 us (14%)
  between operations  15.3 us (9%)
  other arithmetic  13 us (8%)
  starting transfers between devices  3.46 us (2%)
    unnamed x2, waiting for transfers between devices  20.8 us
    dot_general x1, matrix products, synthesize(): product = jnp.dot(spectrum, table, preferred_element_type=jnp.float32)  15.7 us
    psum x1, blocking collectives, on_device(): owner_sum = lax.psum(partial_owner, ('state', 'sub'))  13.9 us
    unnamed x1, blocking collectives  10.3 us
    slice x4, local copies, waits for them, and re-layouts, turn_select(): mats[0]  8.68 us
    dot_general x4, matrix products, turn_select(): jnp.einsum('lQp,lpC->lQC', mats[1], vectors, precision=lax.Precision.HIGH...  7.41 us
    dot_general x4, matrix products, turn_select(): jnp.einsum('lQp,lpC->lQC', mats[0], vectors, precision=lax.Precision.HIGH...  7.38 us
    reshape x4, local copies, waits for them, and re-layouts, turn_select(): complex_join(first, second, width // 2).reshape(degrees, 8, orders, width)  6.15 us
  transfers between devices with their start and end apart: 2, of which 2 were waited for; matrix products, arithmetic and copies ran while one was open for 1% of the time, Pallas kernels for 0%

commit v1 on v0

--- a/solution.py
+++ b/solution.py
@@ -193,7 +193,7 @@
         axial_one,
         axial_two,
     )
-    owner_sum = lax.psum(partial_owner, ("state", "sub"))
+    owner_sum = lax.all_gather(partial_owner, ("state", "sub")).sum(axis=0)
     framed = owner_frame(owner_sum, owner_rotation[0], owner_axial[0])
     leaf_size = lax.axis_size("leaf")
     orders = turn_table.shape[3]

time: 173 us -> 168 us (0.971)
  blocking collectives: 24.2 us -> 18.2 us
    psum x1 -> x0, blocking collectives: 13.9 us -> none  [on_device(): owner_sum = lax.psum(partial_owner, ('state', 'sub'))]
    all_gather x0 -> x1, blocking collectives: none -> 7.92 us  [on_device(): owner_sum = lax.all_gather(partial_owner, ('state', 'sub')).sum(axis=0)]
where the time goes in v1:
time: 168 us; the launch traced here: 165 us
  local copies, waits for them, and re-layouts  50.4 us (30%)
  matrix products  37.5 us (22%)
  waiting for transfers between devices  26.7 us (16%)
  blocking collectives  18.2 us (11%)
  between operations  15.3 us (9%)
  other arithmetic  13 us (8%)
  starting transfers between devices  3.46 us (2%)
    unnamed x2, waiting for transfers between devices  21.4 us
    dot_general x1, matrix products, synthesize(): product = jnp.dot(spectrum, table, preferred_element_type=jnp.float32)  15.7 us
    unnamed x1, blocking collectives  10.3 us
    slice x4, local copies, waits for them, and re-layouts, turn_select(): mats[0]  8.68 us
    all_gather x1, blocking collectives, on_device(): owner_sum = lax.all_gather(partial_owner, ('state', 'sub')).sum(axis=0)  7.92 us
    dot_general x4, matrix products, turn_select(): jnp.einsum('lQp,lpC->lQC', mats[1], vectors, precision=lax.Precision.HIGH...  7.41 us
    dot_general x4, matrix products, turn_select(): jnp.einsum('lQp,lpC->lQC', mats[0], vectors, precision=lax.Precision.HIGH...  7.38 us
    reshape x4, local copies, waits for them, and re-layouts, turn_select(): complex_join(first, second, width // 2).reshape(degrees, 8, orders, width)  6.15 us
  transfers between devices with their start and end apart: 2, of which 2 were waited for; matrix products, arithmetic and copies ran while one was open for 1% of the time, Pallas kernels for 0%

profile of v1, /device:TPU:0, one launch (start us, length us, event | category | flops | bytes accessed | tf_op | source)
XLA Modules:
  0.0 164.6 jit_solution(15084361476817842665)
XLA Ops:
  6.5 0.6 fusion.33
  7.1 4.5 %fusion.46 = (f32[1,12,8,25,25]{4,0,3,1,2:T(1,128)S(1)}, f32[1,12,8,25,25]{4,0,3,1,2:T(1,128)S(1)}) fusion(f32[2,12,8,25,25]{4,0,3,1,2:T(2,128)} %bitcast.183), kind=kLoop, calls=%fused_computation.129 | loop fusion | bytes 960000 | tf_op jit(solution)/shard_map/slice | solution.py:27
  11.7 2.4 %copy.163 = f32[1,12,8,25,25]{3,2,4,1,0:T(8,128)} copy(f32[1,12,8,25,25]{4,0,3,1,2:T(1,128)S(1)} %get-tuple-element.12) | data formatting | bytes 480000 | tf_op jit(solution)/shard_map/slice | solution.py:28
  14.1 2.4 %squeeze.61 = f32[12,200,25]{1,2,0:T(8,128)} reshape(f32[1,12,8,25,25]{3,2,4,1,0:T(8,128)} %copy.163) | data formatting | bytes 480000 | tf_op jit(solution)/shard_map/squeeze | solution.py:28
  17.4 0.7 mul.178
  18.1 2.6 %reshape.344 = bf16[300,1024]{1,0:T(8,128)(2,1)S(1)} reshape(bf16[12,25,2,2,4,64]{5,4,3,2,1,0:T(4,128)(2,1)} %param.14) | data formatting | bytes 1228800 | tf_op jit(solution)/shard_map/reshape | solution.py:78
  21.2 1.1 copy.162
  22.7 3.3 %convolution_bitcast_fusion.2 = f32[12,200,256]{2,1,0:T(8,128)S(1)} fusion(f32[12,25,256]{2,1,0:T(8,128)S(1)} %reshape.345, f32[12,200,25]{1,2,0:T(8,128)} %squeeze.61), kind=kOutput, calls=%fused_computation.26 | convolution fusion | flops 184320000 | bytes 3004800 | tf_op jit(solution)/shard_map/lQp,lpC->lQC/dot_general | solution.py:28
  26.0 2.2 %convolution_bitcast_fusion.3 = f32[12,200,256]{2,1,0:T(8,128)S(1)} fusion(f32[12,25,256]{2,1,0:T(8,128)S(1)} %reshape.345, f32[12,200,25]{1,2,0:T(8,128)S(1)} %squeeze.60), kind=kOutput, calls=%fused_computation.27 | convolution fusion | flops 184320000 | bytes 3004800 | tf_op jit(solution)/shard_map/lQp,lpC->lQC/dot_general | solution.py:27
  28.4 1.6 pad_maximum_fusion
  30.1 2.5 %reshape.346 = f32[12,8,25,256]{3,2,1,0:T(8,128)S(1)} reshape(f32[12,200,256]{2,1,0:T(8,128)} %pad_maximum_fusion) | data formatting | bytes 4915200 | tf_op jit(solution)/shard_map/reshape | solution.py:29
  32.5 0.7 fusion.37
  33.2 0.6 tile.8
  33.8 1.5 tile.9
  35.4 1.9 %multiply_reduce_fusion.1 = f32[12,25,256]{2,1,0:T(8,128)} fusion(f32[12,8,25,256]{3,2,1,0:T(8,128)S(1)} %reshape.346, f32[8,256]{1,0:T(8,128)} %tile.9), kind=kLoop, calls=%fused_computation.13 | loop fusion | flops 1152000 | bytes 2772992 | tf_op jit(solution)/shard_map/reduce_sum | solution.py:33
  37.2 1.4 reshape.347
  39.4 0.7 copy.206
  40.4 1.1 copy.205
  41.8 0.6 convolution_bitcast_fusion.8
  42.5 0.6 convolution_bitcast_fusion.9
  43.5 1.2 reshape.349
  44.7 2.2 %copy.169 = f32[12,25,2,2,64]{4,3,2,1,0:T(2,128)} copy(f32[12,25,2,2,64]{4,2,0,3,1:T(2,128)} %bitcast.185) | data formatting | bytes 614400 | tf_op jit(solution)/shard_map/transpose | solution.py:45
  46.9 1.5 reshape.350
  48.4 2.9 %fusion.45 = (f32[1,12,8,25,25]{3,0,4,1,2:T(1,128)S(1)}, f32[1,12,8,25,25]{3,0,4,1,2:T(1,128)}) fusion(f32[2,12,8,25,25]{3,0,4,1,2:T(2,128)S(1)} %bitcast.184), kind=kLoop, calls=%fused_computation.128 | loop fusion | bytes 960000 | tf_op jit(solution)/shard_map/slice | solution.py:27
  51.5 1.1 squeeze.64
  53.1 3.3 %convolution_bitcast_fusion.1 = f32[12,200,256]{2,1,0:T(8,128)S(1)} fusion(f32[12,25,256]{2,1,0:T(8,128)S(1)} %reshape.350, f32[12,200,25]{1,2,0:T(8,128)} %squeeze.64), kind=kOutput, calls=%fused_computation.25 | convolution fusion | flops 184320000 | bytes 3004800 | tf_op jit(solution)/shard_map/lQp,lpC->lQC/dot_general | solution.py:27
  56.5 2.2 %multiply_bitcast_fusion = f32[12,200,256]{2,1,0:T(8,128)S(1)} fusion(f32[12,25,256]{2,1,0:T(8,128)S(1)} %reshape.350, f32[12,200,25]{1,2,0:T(8,128)S(1)} %squeeze.65), kind=kOutput, calls=%fused_computation.16 | convolution fusion | flops 184934400 | bytes 3004800 | tf_op jit(solution)/shard_map/lQp,lpC->lQC/dot_general | solution.py:28
  58.9 1.6 pad_maximum_fusion.1
  60.5 2.6 %reshape.351 = f32[12,8,25,256]{3,2,1,0:T(8,128)S(1)} reshape(f32[12,200,256]{2,1,0:T(8,128)} %pad_maximum_fusion.1) | data formatting | bytes 4915200 | tf_op jit(solution)/shard_map/reshape | solution.py:29
  63.2 1.9 %multiply_reduce_fusion = f32[12,25,256]{2,1,0:T(8,128)} fusion(f32[12,8,25,256]{3,2,1,0:T(8,128)S(1)} %reshape.351, f32[8,256]{1,0:T(8,128)} %tile.9), kind=kLoop, calls=%fused_computation.12 | loop fusion | flops 1152000 | bytes 2772992 | tf_op jit(solution)/shard_map/reduce_sum | solution.py:33
  65.3 2.0 %fusion.51 = f32[12,25,32]{1,2,0:T(8,128)S(1)} fusion(f32[12,25,256]{2,1,0:T(8,128)} %multiply_reduce_fusion, f32[256,32,1]{0,1,2:T(8,128)S(1)} %reshape.366), kind=kOutput, calls=%fused_computation.136 | convolution fusion | flops 29491200 | bytes 378368 | tf_op jit(solution)/shard_map/lpC,CD->lpD/dot_general | solution.py:91
  67.3 1.5 convolution_bitcast_fusion.6
  68.8 1.5 convolution_bitcast_fusion.5
  70.4 0.5 reshape.352
  71.0 0.5 multiply_reduce_fusion.3
  71.8 0.7 copy.208
  72.8 0.7 copy.207
  73.8 0.6 convolution_bitcast_fusion.10
  74.4 0.6 convolution_bitcast_fusion.11
  75.3 0.5 convolution_bitcast_fusion.4
  75.8 0.5 fusion.15
  76.4 0.5 reshape.357
  76.9 0.5 multiply_reduce_fusion.2
  77.7 7.9 %all-gather = f32[48,25,16]{1,2,0:T(8,128)S(1)} all-gather(f32[12,25,16]{1,2,0:T(8,128)S(1)} %reduce_sum.58), channel_id=2, replica_groups=mesh['groups'=2,'leaf'=4,'state'=2,'sub'=2] {'state','sub'}, dimensions={0}, use_global_device_ids=true | all-gather | bytes 96000 | tf_op jit(solution)/shard_map/all_gather | solution.py:196
  85.6 1.4 fusion.50
  87.0 0.4 convolution_bitcast_fusion.14
  87.4 0.4 convolution_bitcast_fusion.15
  89.9 0.4 convolution_bitcast_fusion.13
  91.5 0.6 dynamic_slice.3
  92.1 0.7 fusion.38
  92.9 1.0 copy.210
  93.9 0.8 copy.195
  94.7 0.6 dynamic-slice
  95.3 21.3 %reduce-scatter.4.cloned.1.call-done = f32[64,512]{1,0:T(8,128)} async-done(((f32[256,512]{1,0:T(8,128)}), f32[64,512]{1,0:T(8,128)}) %reduce-scatter.4.cloned.1.call-update) | async-done | bytes 131088
  116.7 1.0 copy.211
  119.1 10.3 %all-reduce = bf16[4,4,1024]{2,1,0:T(4,128)(2,1)S(1)} all-reduce(bf16[4,4,1024]{2,1,0:T(4,128)(2,1)S(1)} %copy.209), channel_id=4, replica_groups=mesh['groups'=2,'leaf'=4,'state'=2,'sub'=2] {'state','sub'}, use_global_device_ids=true, to_apply=%region_7.8.clone | all-reduce | flops 16384 | bytes 65536
  129.3 0.7 constant_dynamic-slice_fusion
  130.0 0.5 broadcast.208
  130.6 0.7 reduce.2
  131.2 0.6 reshape.378
  131.9 3.5 %all-to-all-start = ((bf16[4,2,512]{2,1,0:T(2,128)(2,1)}), bf16[4,2,512]{2,1,0:T(2,128)(2,1)S(1)}, u32[]{:S(2)}, u32[]{:S(2)}) async-start(bf16[4,2,512]{2,1,0:T(2,128)(2,1)} %reshape.378), calls=%async_computation | async-start | bytes 16384 | tf_op jit(solution)/shard_map/all_to_all | solution.py:222
  135.3 5.3 %all-to-all-done = bf16[4,2,512]{2,1,0:T(2,128)(2,1)S(1)} async-done(((bf16[4,2,512]{2,1,0:T(2,128)(2,1)}), bf16[4,2,512]{2,1,0:T(2,128)(2,1)S(1)}, u32[]{:S(2)}, u32[]{:S(2)}) %all-to-all-start) | async-done | bytes 8224 | tf_op jit(solution)/shard_map/all_to_all | solution.py:222
  140.9 15.7 %convolution_bitcast_fusion = f32[2,2,4,1,4096]{4,2,1,0,3:T(4,128)S(1)} fusion(bf16[2,2,4,256]{3,2,1,0:T(4,128)(2,1)S(1)} %dot_general.132, f32[4096]{0:T(1024)S(1)} %fusion.28, s32[4096]{0:T(1024)S(1)} %add_select_fusion.2, s32[256]{0:T(256)S(1)} %iota_add_fusion), kind=kOutput, calls=%fused_computation.5 | convolution fusion | flops 50331648 | bytes 304128 | tf_op jit(solution)/shard_map/dot_general | solution.py:161
  156.7 0.8 copy.202
  (114 shorter events, 10.7 us)
Async XLA Ops:
  6.5 84.2 %copy-start = (bf16[1,32,25,256]{3,1,2,0:T(8,128)(2,1)S(1)}, bf16[1,32,25,256]{3,1,2,0:T(8,128)(2,1)}, u32[]{:S(2)}) copy-start(bf16[1,32,25,256]{3,1,2,0:T(8,128)(2,1)} %param.26) | copy-start | bytes 1228804
  6.5 110.1 %reduce-scatter.4.cloned.1.call-start = ((), (), s32[]{:S(2)}) async-start(), calls=%async_computation.2 | async-start | bytes 655360
  11.7 5.5 %copy-start.12 = (s32[64]{0:T(128)S(1)}, s32[64]{0:T(128)}, u32[]{:S(2)}) copy-start(s32[64]{0:T(128)} %param.16) | copy-start | bytes 772
  22.7 5.5 %copy-start.3 = (f32[12,200,25]{1,2,0:T(8,128)}, f32[12,200,25]{1,2,0:T(8,128)S(1)}, u32[]{:S(2)}) copy-start(f32[12,200,25]{1,2,0:T(8,128)S(1)} %squeeze.60) | copy-start | bytes 720004
  37.2 2.1 %copy-start.8 = (f32[2,25,2,12,2,12]{1,4,5,3,2,0:T(2,128)S(1)}, f32[2,25,2,12,2,12]{1,4,5,3,2,0:T(2,128)}, u32[]{:S(2)}) copy-start(f32[2,25,2,12,2,12]{1,4,5,3,2,0:T(2,128)} %param.21) | copy-start | bytes 345604
  43.3 5.1 %copy-start.1 = (f32[8,2,12,25,25]{4,1,3,2,0:T(2,128)S(1)}, f32[8,2,12,25,25]{4,1,3,2,0:T(2,128)}, u32[]{:S(2)}) copy-start(f32[8,2,12,25,25]{4,1,3,2,0:T(2,128)} %param.20) | copy-start | bytes 1440004
  51.4 1.3 copy-start.2
  53.1 5.5 %copy-start.5 = (f32[12,200,25]{1,2,0:T(8,128)}, f32[12,200,25]{1,2,0:T(8,128)S(1)}, u32[]{:S(2)}) copy-start(f32[12,200,25]{1,2,0:T(8,128)S(1)} %squeeze.65) | copy-start | bytes 720004
  63.2 1.9 %copy-start.13 = (s32[16]{0:T(128)S(1)}, s32[16]{0:T(128)}, u32[]{:S(2)}) copy-start(s32[16]{0:T(128)} %param.17) | copy-start | bytes 196
  63.2 1.9 %copy-start.11 = (f32[16,16]{0,1:T(8,128)S(1)}, f32[16,16]{0,1:T(8,128)}, u32[]{:S(2)}) copy-start(f32[16,16]{0,1:T(8,128)} %fusion.33) | copy-start | bytes 3076
  68.8 2.1 %copy-start.14 = (s32[2]{0:T(128)S(1)}, s32[2]{0:T(128)}, u32[]{:S(2)}) copy-start(s32[2]{0:T(128)} %param.19) | copy-start | bytes 28
  70.4 1.4 copy-start.9
  72.8 2.5 %copy-start.4 = (f32[12,200,25]{1,2,0:T(8,128)S(1)}, f32[12,200,25]{1,2,0:T(8,128)}, u32[]{:S(2)}) copy-start(f32[12,200,25]{1,2,0:T(8,128)} %squeeze.64) | copy-start | bytes 720004
  73.5 2.3 %copy-start.6 = (f32[12,200,25]{1,2,0:T(8,128)S(1)}, f32[12,200,25]{1,2,0:T(8,128)}, u32[]{:S(2)}) copy-start(f32[12,200,25]{1,2,0:T(8,128)} %copy-done.5) | copy-start | bytes 720004
  76.9 11.2 %copy-start.7 = (f32[1,2,25,2,32,2,12]{4,5,6,3,2,1,0:T(2,128)S(1)}, f32[1,2,25,2,32,2,12]{4,5,6,3,2,1,0:T(2,128)}, u32[]{:S(2)}) copy-start(f32[1,2,25,2,32,2,12]{4,5,6,3,2,1,0:T(2,128)} %param.24) | copy-start | bytes 921604
  89.2 2.3 %copy-start.15 = (f32[4]{0:T(128)S(1)}, f32[4]{0:T(128)}, u32[]{:S(2)}) copy-start(f32[4]{0:T(128)} %param.25) | copy-start | bytes 52
  91.1 2.8 %copy-start.10 = (bf16[64,32,32]{0,2,1:T(8,128)(2,1)S(1)}, bf16[64,32,32]{0,2,1:T(8,128)(2,1)}, u32[]{:S(2)}) copy-start(bf16[64,32,32]{0,2,1:T(8,128)(2,1)} %param.27) | copy-start | bytes 393220
  91.4 3.3 %copy-start.16 = (u32[32]{0:T(128)S(1)}, u32[32]{0:T(128)}, u32[]{:S(2)}) copy-start(u32[32]{0:T(128)} %constant.84) | copy-start | bytes 388
  131.9 8.8 %all-to-all-start = ((bf16[4,2,512]{2,1,0:T(2,128)(2,1)}), bf16[4,2,512]{2,1,0:T(2,128)(2,1)S(1)}, u32[]{:S(2)}, u32[]{:S(2)}) async-start(bf16[4,2,512]{2,1,0:T(2,128)(2,1)} %reshape.378), calls=%async_computation | async-start | bytes 16384 | tf_op jit(solution)/shard_map/all_to_all | solution.py:222
Sparse Core Ops, SparseCore 0:
  94.0 22.5 reduce-scatter.3
